TPU v7x, 32 devices: a whole 2x2x4 slice. The times are simulated.
32 devices in a mesh: grid: 8 (over z, x), mem: 4 (over y, core).
Axes of the slice: x: 2, y: 2, z: 4, core: 2. Of those that a mesh axis runs over, the one named last changes fastest.
Arguments:
- members: bfloat16 [80, 4, 16, 512], P('mem', None, 'grid'), may hold values from -0.8984375 to 0.8984375
- innovation: float32 [4, 16, 512], P(None, 'grid'), may hold values from -6 to 6
- observed_count: int32 [16, 512], P('grid'), may hold values from 0 to 3
- obs_precision: float32 [4], replicated, may hold values from 0.5 to 4
Outputs:
- recentred: bfloat16 [80, 4, 16, 512], P('mem', None, 'grid')
- increment: float32 [4, 16, 512], P('mem', 'grid')
All inputs are finite; a program needn't handle non-finite values.
Results may differ from a plain program's by a relative error of at most 0.0004.
Values may be sent and summed in bfloat16 or wider, within the bound.
No kernel may reach another device: no remote copies, remote signals or barrier semaphores. Data moves between devices by JAX's collectives and lax.ppermute only.
A program may use at most 64 MiB of HBM per device.

v0:
```python
import jax
import jax.numpy as jnp
from jax import lax
from jax.sharding import PartitionSpec as P

PASSES = 2
ITERS = 2
diffusion = 0.25


def padded(value, sides, width):
    for axis, dim in sides:
        devices, length = (lax.axis_size(axis), value.shape[dim])
        up = [(i, (i + 1) % devices) for i in range(devices - 1)]
        down = [(j, i) for i, j in up]
        last = lax.slice_in_dim(value, length - width, length, axis=dim)
        leading = lax.slice_in_dim(value, 0, width, axis=dim)
        before = lax.ppermute(last, axis, up)
        after = lax.ppermute(leading, axis, down)
        value = jnp.concatenate([before, value, after], axis=dim)
    return value


def smooth(field):
    for sweep_index in range(PASSES):
        extended = padded(field, (("grid", 2),), 1)
        centre = extended[:, :, 1:-1]
        field = centre + diffusion * (extended[:, :, :-2] + extended[:, :, 2:] - 2.0 * centre)
    for sweep_index in range(PASSES):
        field = field + diffusion * (jnp.roll(field, 1, 3) + jnp.roll(field, -1, 3) - 2.0 * field)
    return field


def member_total(product):
    summed = jnp.sum(product, axis=0)
    return summed


def norm_of(residual):
    return lax.psum(jnp.sum(residual * residual), ("grid", "mem"))


def local(members, innovation, observed_count, obs_precision):
    mem_index = lax.axis_index("mem")
    level_share = members.shape[1] // lax.axis_size("mem")
    perturbed = lax.all_to_all(members, "mem", split_axis=1, concat_axis=0, tiled=True)
    precision = lax.dynamic_slice_in_dim(obs_precision, mem_index * level_share, level_share, 0)
    local_innovation = lax.dynamic_slice_in_dim(innovation, mem_index * level_share, level_share, 0)
    weight = observed_count.astype(jnp.float32)[None] * precision[:, None, None]
    gradient = smooth(perturbed * (weight * local_innovation)[None])
    carried = jnp.zeros_like(gradient)
    residual = gradient
    direction = residual
    norm_now = norm_of(residual)
    for iteration in range(ITERS):
        smoothed = smooth(direction)
        total = member_total(perturbed * smoothed)
        back = smooth(perturbed * (weight * total)[None])
        image, smoothed = (direction + back, smoothed)
        step_size = norm_now / lax.psum(jnp.sum(direction * image), ("grid", "mem"))
        carried = carried + step_size * smoothed
        residual = residual - step_size * image
        if iteration + 1 < ITERS:
            norm_next = norm_of(residual)
            direction = residual + norm_next / norm_now * direction
            norm_now = norm_next
    increment = member_total(perturbed * carried)
    whole = lax.all_gather(increment, "mem", axis=0, tiled=True)
    recentred = (members.astype(jnp.float32) + whole[None]).astype(jnp.bfloat16)
    return (recentred, increment)


def smooth_rows(field):
    nlat = field.shape[-2]
    row = lax.broadcasted_iota(jnp.int32, (nlat, 1), 0)
    centre = jnp.where((row == 0) | (row == nlat - 1), 0.3125, 0.375)
    wide = jnp.pad(field, [(0, 0)] * (field.ndim - 2) + [(2, 2), (0, 0)])
    near = lax.slice_in_dim(wide, 1, nlat + 1, axis=-2) + lax.slice_in_dim(
        wide, 3, nlat + 3, axis=-2
    )
    far = lax.slice_in_dim(wide, 0, nlat, axis=-2) + lax.slice_in_dim(wide, 4, nlat + 4, axis=-2)
    field = centre * field + 0.25 * near + 0.0625 * far
    nlon = field.shape[-1]
    wide = jnp.concatenate([field[..., nlon - 2 :], field, field[..., :2]], axis=-1)
    near = wide[..., 1 : nlon + 1] + wide[..., 3 : nlon + 3]
    far = wide[..., :nlon] + wide[..., 4 : nlon + 4]
    return 0.375 * field + 0.25 * near + 0.0625 * far


def exchange(values, rows_for, width=128):
    devices = lax.axis_size("grid") * lax.axis_size("mem")
    nlon = rows_for.shape[-1]
    rows = rows_for.shape[1]
    lanes = [jnp.sum(v.reshape(-1, width), axis=0) for v in values]
    head = jnp.broadcast_to(jnp.concatenate(lanes), (devices, width * len(values)))
    parcel = jnp.concatenate([head, rows_for.reshape(devices, rows * nlon)], axis=1)
    got = lax.all_to_all(parcel, ("grid", "mem"), 0, 0, tiled=True)
    parts = jnp.sum(got[:, : width * len(values)].reshape(devices, len(values), width), axis=0)
    sums = jnp.dot(parts, jnp.ones((width, 128), jnp.float32), precision=lax.Precision.HIGHEST)
    received = got[:, width * len(values) :].reshape(devices, rows, nlon)
    return ([jnp.tile(sums[i : i + 1], (1, nlon // 128)) for i in range(len(values))], received)


def mem_total(part):
    mem_size = lax.axis_size("mem")
    got = lax.all_to_all(jnp.broadcast_to(part, (mem_size,) + part.shape), "mem", 0, 0, tiled=True)
    return jnp.sum(got, axis=0)


def local_by_level(members, innovation, observed_count, obs_precision):
    grid_size = lax.axis_size("grid")
    mem_size = lax.axis_size("mem")
    count, levels, rows, nlon = members.shape
    copies = grid_size // levels
    nlat = rows * grid_size
    grid_index = lax.axis_index("grid")
    mem_index = lax.axis_index("mem")
    level = grid_index // copies
    counts = jnp.broadcast_to(observed_count.astype(jnp.bfloat16), (1, levels, rows, nlon))
    high = lax.reduce_precision(innovation, exponent_bits=8, mantissa_bits=7)
    rest = innovation - high
    middle = lax.reduce_precision(rest, exponent_bits=8, mantissa_bits=7)
    low = rest - middle
    parts = jnp.stack([high, middle, low]).astype(jnp.bfloat16)
    packed = jnp.repeat(jnp.concatenate([members, counts, parts], axis=0), copies, axis=1)
    got = lax.all_to_all(packed, "grid", 1, 2, tiled=True)[:, 0]
    split = got[count + 1 :].astype(jnp.float32)
    innov = split[0] + split[1] + split[2]
    precision = lax.dynamic_index_in_dim(obs_precision, level, 0, keepdims=False)
    weight = got[count].astype(jnp.float32) * precision
    widened = lax.optimization_barrier(got[:count]).astype(jnp.float32)
    span = nlat // copies
    own = lax.broadcasted_iota(jnp.int32, (nlat, nlon), 0) // span == grid_index % copies
    first = mem_index == 0
    half = grid_index % copies

    def own_rows(field):
        return lax.dynamic_slice_in_dim(field, half * span, span, axis=1)

    def squares(field):
        mine = own_rows(field)
        return jnp.sum(mine * mine, axis=(0, 1))

    def weighted(total):
        mine = lax.dynamic_slice_in_dim(total, half * span, span, axis=0)
        scale = lax.dynamic_slice_in_dim(weight, half * span, span, axis=0)
        return jnp.where(first, jnp.sum(scale * mine * mine, axis=0), 0.0)

    def by_target(field):
        return jnp.repeat(field.reshape(grid_size, rows, nlon), mem_size, axis=0)

    residual = smooth_rows(widened * (weight * innov)[None])
    total1 = mem_total(jnp.sum(widened * smooth_rows(residual), axis=0))
    image = residual + smooth_rows(widened * (weight * total1)[None])
    image_part = jnp.sum(widened * smooth_rows(image), axis=0)
    if copies > 1:
        rows_for = jnp.where(grid_index % copies == 0, by_target(total1), by_target(image_part))
    else:
        rows_for = jnp.concatenate([by_target(total1), by_target(image_part)], axis=1)
    sums1, got1 = exchange([squares(residual), weighted(total1)], rows_for)
    norm_now = sums1[0]
    curvature1 = sums1[1]
    step1 = norm_now / (norm_now + curvature1)
    if copies > 1:
        by_source = got1.reshape(levels, copies, mem_size, rows, nlon)
        total1_rows = by_source[:, 0, 0]
        image_rows = jnp.sum(by_source[:, 1], axis=1)
    else:
        by_source = got1.reshape(levels, mem_size, 2 * rows, nlon)
        total1_rows = by_source[:, 0, :rows]
        image_rows = jnp.sum(by_source[:, :, rows:], axis=1)
    residual_next = residual - step1 * image
    weight_rows = observed_count.astype(jnp.float32)[None] * obs_precision[:, None, None]
    moved_rows = total1_rows - step1 * image_rows
    sums, _ = exchange(
        [
            squares(residual_next),
            jnp.sum(own_rows(residual_next) * own_rows(residual), axis=(0, 1)),
            jnp.where(first, jnp.sum(weight_rows * moved_rows * moved_rows, axis=(0, 1)), 0.0),
            jnp.where(first, jnp.sum(weight_rows * moved_rows * total1_rows, axis=(0, 1)), 0.0),
        ],
        jnp.zeros((grid_size * mem_size, 0, nlon), jnp.float32),
        width=128,
    )
    norm_next = sums[0]
    beta = norm_next / norm_now
    direction_sq = norm_next + 2.0 * beta * sums[1] + beta * beta * norm_now
    curvature2 = sums[2] + 2.0 * beta * sums[3] + beta * beta * curvature1
    step2 = norm_next / (direction_sq + curvature2)
    total2_rows = moved_rows + beta * total1_rows
    whole = step1 * total1_rows + step2 * total2_rows
    share = levels // mem_size
    mine_out = lax.dynamic_slice_in_dim(whole, mem_index * share, share, 0)
    recentred = (members.astype(jnp.float32) + whole[None]).astype(jnp.bfloat16)
    return (recentred, mine_out)


def solution(mesh):
    placed = (P("mem", None, "grid", None), P(None, "grid", None), P("grid", None), P())
    grid_size, mem_size = (mesh.shape["grid"], mesh.shape["mem"])
    body = local

    def chosen(members, innovation, observed_count, obs_precision):
        levels = members.shape[1]
        fits = (
            grid_size % levels == 0
            and grid_size // levels <= 2
            and (levels % mem_size == 0)
            and (ITERS == 2)
        )
        pick = local_by_level if fits else body
        return jax.shard_map(
            pick,
            mesh=mesh,
            in_specs=placed,
            out_specs=(P("mem", None, "grid", None), P("mem", "grid", None)),
            check_vma=False,
        )(members, innovation, observed_count, obs_precision)

    return chosen
```

profile of v0, /device:TPU:0, one launch (start us, length us, event | category | flops | bytes accessed | tf_op | source)
XLA Modules:
  0.0 62.8 jit_solution(13325547275627384999)
XLA Ops:
  0.6 0.8 %fusion.80 = (bf16[2,512]{1,0:T(2,128)(2,1)S(1)}, f32[2,512]{1,0:T(2,128)S(1)}) fusion(s32[2,512]{1,0:T(2,128)} %param.6), kind=kLoop, calls=%fused_computation.179 | loop fusion | flops 2048 | bytes 10240 | tf_op jit(solution)/shard_map/convert_element_type | solution.py:119
  1.4 1.0 %constant_dynamic-update-slice_fusion.4 = bf16[24,4,2,512]{3,2,1,0:T(2,128)(2,1)S(1)} fusion(bf16[20,4,2,512]{3,2,1,0:T(2,128)(2,1)} %param.4), kind=kLoop, calls=%fused_computation.140 | loop fusion | bytes 327680
  2.5 0.1 copy.11
  2.7 0.9 %broadcast_in_dim.56 = bf16[24,4,2,2,512]{4,3,0,2,1:T(2,128)(2,1)} broadcast(bf16[24,4,2,512]{3,2,0,1:T(2,128)(2,1)S(1)} %copy.11), dimensions={0,1,3,4} | broadcast | bytes 589824 | tf_op jit(solution)/shard_map/broadcast_in_dim | solution.py:125
  3.6 7.3 %all-to-all-start = ((bf16[24,8,2,512]{3,2,0,1:T(2,128)(2,1)}), bf16[24,8,2,512]{3,2,0,1:T(2,128)(2,1)S(1)}, u32[]{:S(2)}, u32[]{:S(2)}) async-start(bf16[24,8,2,512]{3,2,0,1:T(2,128)(2,1)} %bitcast.3), calls=%async_computation | async-start | bytes 786432 | tf_op jit(solution)/shard_map/all_to_all | solution.py:126
  10.9 0.6 %copy-done.2 = f32[4]{0:T(128)S(1)} copy-done((f32[4]{0:T(128)S(1)}, f32[4]{0:T(128)}, u32[]{:S(2)}) %copy-start.2) | copy-done | bytes 40
  11.6 0.6 dynamic_slice.21
  12.2 10.4 %all-to-all-done = bf16[24,8,2,512]{3,2,0,1:T(2,128)(2,1)S(1)} async-done(((bf16[24,8,2,512]{3,2,0,1:T(2,128)(2,1)}), bf16[24,8,2,512]{3,2,0,1:T(2,128)(2,1)S(1)}, u32[]{:S(2)}, u32[]{:S(2)}) %all-to-all-start) | async-done | bytes 393248 | tf_op jit(solution)/shard_map/all_to_all | solution.py:126
  22.6 0.2 slice.250
  22.8 0.3 copy.12
  23.1 0.1 slice.194
  23.3 0.7 %convert_multiply_fusion.4 = (f32[1,8,2,512]{3,2,0,1:T(2,128)S(1)}, f32[1,8,2,512]{3,2,0,1:T(2,128)S(1)}) fusion(bf16[24,8,2,512]{3,2,0,1:T(2,128)(2,1)S(1)} %all-to-all-done, f32[]{:T(128)} %bitcast.4, f32[3,8,2,512]{3,2,0,1:T(2,128)S(1)} %slice_convert_fusion), kind=kLoop, calls=%fused_computation.117 | loop fusion | flops 40960 | bytes 180228 | tf_op jit(solution)/shard_map/mul | solution.py:130
  24.2 0.3 fusion.28
  24.6 0.9 %fusion.23 = f32[20,16,512]{2,1,0:T(8,128)S(1)} fusion(f32[20,16,512]{2,1,0:T(8,128)S(1)} %fusion.28, f32[20,16,2]{2,1,0:T(8,128)S(1)} %get-tuple-element.14, f32[20,16,2]{2,1,0:T(8,128)S(1)} %get-tuple-element.13), kind=kLoop, calls=%fused_computation.59 | loop fusion | flops 1802240 | bytes 1315840 | tf_op jit(solution)/shard_map/add | solution.py:87
  25.5 0.3 fusion.34
  26.0 0.9 %fusion.57 = f32[16,512]{1,0:T(8,128)S(1)} fusion(f32[20,16,2]{2,1,0:T(8,128)S(1)} %get-tuple-element.12, f32[20,16,512]{2,1,0:T(8,128)S(1)} %fusion.34, f32[20,16,2]{2,1,0:T(8,128)S(1)} %get-tuple-element.11, bf16[20,16,512]{2,1,0:T(8,128)(2,1)S(1)} %slice.194), kind=kLoop, calls=%fused_computation.101 | loop fusion | flops 2285568 | bytes 1020928 | tf_op jit(solution)/shard_map/reduce_sum | solution.py:153
  26.9 0.7 %broadcast_in_dim.57 = f32[4,16,512]{2,1,0:T(8,128)} broadcast(f32[16,512]{1,0:T(8,128)S(1)} %fusion.57), dimensions={1,2} | broadcast | bytes 163840 | tf_op jit(solution)/shard_map/broadcast_in_dim | solution.py:106
  27.5 3.3 %all-to-all-start.1 = ((f32[4,16,512]{2,1,0:T(8,128)}), f32[4,16,512]{2,1,0:T(8,128)S(1)}, u32[]{:S(2)}, u32[]{:S(2)}) async-start(f32[4,16,512]{2,1,0:T(8,128)} %broadcast_in_dim.57), calls=%async_computation.1 | async-start | bytes 262144 | tf_op jit(solution)/shard_map/all_to_all | solution.py:106
  30.9 4.5 %all-to-all-done.1 = f32[4,16,512]{2,1,0:T(8,128)S(1)} async-done(((f32[4,16,512]{2,1,0:T(8,128)}), f32[4,16,512]{2,1,0:T(8,128)S(1)}, u32[]{:S(2)}, u32[]{:S(2)}) %all-to-all-start.1) | async-done | bytes 131104 | tf_op jit(solution)/shard_map/all_to_all | solution.py:106
  35.6 0.3 fusion.40
  36.0 0.9 %fusion.11 = f32[20,16,512]{2,1,0:T(8,128)S(1)} fusion(f32[20,16,512]{2,1,0:T(8,128)S(1)} %fusion.23, f32[20,16,512]{2,1,0:T(8,128)S(1)} %fusion.40, f32[20,16,2]{2,1,0:T(8,128)S(1)} %get-tuple-element.10, f32[20,16,2]{2,1,0:T(8,128)S(1)} %get-tuple-element.9), kind=kLoop, calls=%fused_computation.47 | loop fusion | flops 1966080 | bytes 1971200 | tf_op jit(solution)/shard_map/add | solution.py:154
  36.9 0.3 fusion.46
  37.4 0.9 %fusion.58 = f32[16,512]{1,0:T(8,128)S(1)} fusion(f32[20,16,2]{2,1,0:T(8,128)S(1)} %get-tuple-element.8, f32[20,16,512]{2,1,0:T(8,128)S(1)} %fusion.46, f32[20,16,2]{2,1,0:T(8,128)S(1)} %get-tuple-element.7, bf16[20,16,512]{2,1,0:T(8,128)(2,1)S(1)} %slice.194), kind=kLoop, calls=%fused_computation.102 | loop fusion | flops 2285568 | bytes 1020928 | tf_op jit(solution)/shard_map/reduce_sum | solution.py:155
  38.4 0.1 all_to_all.24
  38.5 11.2 %all_to_all.32 = f32[32,1,1280]{2,1,0:T(1,128)S(1)} all-to-all(f32[32,1,1280]{2,1,0:T(1,128)S(1)} %all_to_all.24), channel_id=1, replica_groups=mesh['grid'=8,'mem'=4] {'grid','mem'}, dimensions={0} | all-to-all | bytes 327680 | tf_op jit(solution)/shard_map/all_to_all | solution.py:97
  49.9 0.1 fusion.63
  50.3 0.7 %broadcast_in_dim.61 = f32[32,1,512]{2,1,0:T(1,128)} broadcast(f32[512]{0:T(512)S(1)} %pad_maximum_fusion.10), dimensions={2} | broadcast | bytes 67584 | tf_op jit(solution)/shard_map/broadcast_in_dim | solution.py:95
  51.0 2.7 %all-to-all-start.3 = ((f32[32,1,512]{2,1,0:T(1,128)}), f32[32,1,512]{2,1,0:T(1,128)S(1)}, u32[]{:S(2)}, u32[]{:S(2)}) async-start(f32[32,1,512]{2,1,0:T(1,128)} %broadcast_in_dim.61), calls=%async_computation.3 | async-start | bytes 131072 | tf_op jit(solution)/shard_map/all_to_all | solution.py:97
  53.7 7.4 %all-to-all-done.3 = f32[32,1,512]{2,1,0:T(1,128)S(1)} async-done(((f32[32,1,512]{2,1,0:T(1,128)}), f32[32,1,512]{2,1,0:T(1,128)S(1)}, u32[]{:S(2)}, u32[]{:S(2)}) %all-to-all-start.3) | async-done | bytes 65568 | tf_op jit(solution)/shard_map/all_to_all | solution.py:97
  61.2 0.1 fusion.61
  61.4 0.8 %add_convert_fusion = bf16[20,4,2,512]{3,2,1,0:T(2,128)(2,1)} fusion(bf16[20,4,2,512]{3,2,1,0:T(2,128)(2,1)S(1)} %copy-done, f32[4,2,512]{2,1,0:T(2,128)S(1)} %multiply_add_fusion), kind=kLoop, calls=%fused_computation.105 | loop fusion | flops 245760 | bytes 344064 | tf_op jit(solution)/shard_map/convert_element_type | solution.py:194
  62.2 0.6 constant_dynamic-slice_fusion
  (47 shorter events, 1.6 us)
Async XLA Ops:
  1.4 1.1 %copy-start.1 = (f32[4,2,512]{2,1,0:T(2,128)S(1)}, f32[4,2,512]{2,1,0:T(2,128)}, u32[]{:S(2)}) copy-start(f32[4,2,512]{2,1,0:T(2,128)} %param.5) | copy-start | bytes 49156
  3.6 19.0 %all-to-all-start = ((bf16[24,8,2,512]{3,2,0,1:T(2,128)(2,1)}), bf16[24,8,2,512]{3,2,0,1:T(2,128)(2,1)S(1)}, u32[]{:S(2)}, u32[]{:S(2)}) async-start(bf16[24,8,2,512]{3,2,0,1:T(2,128)(2,1)} %bitcast.3), calls=%async_computation | async-start | bytes 786432 | tf_op jit(solution)/shard_map/all_to_all | solution.py:126
  10.9 0.7 %copy-start.2 = (f32[4]{0:T(128)S(1)}, f32[4]{0:T(128)}, u32[]{:S(2)}) copy-start(f32[4]{0:T(128)} %param.7) | copy-start | bytes 52
  27.5 7.9 %all-to-all-start.1 = ((f32[4,16,512]{2,1,0:T(8,128)}), f32[4,16,512]{2,1,0:T(8,128)S(1)}, u32[]{:S(2)}, u32[]{:S(2)}) async-start(f32[4,16,512]{2,1,0:T(8,128)} %broadcast_in_dim.57), calls=%async_computation.1 | async-start | bytes 262144 | tf_op jit(solution)/shard_map/all_to_all | solution.py:106
  51.0 10.4 %copy-start = (bf16[20,4,2,512]{3,2,1,0:T(2,128)(2,1)S(1)}, bf16[20,4,2,512]{3,2,1,0:T(2,128)(2,1)}, u32[]{:S(2)}) copy-start(bf16[20,4,2,512]{3,2,1,0:T(2,128)(2,1)} %param.4) | copy-start | bytes 491524
  51.0 10.1 %all-to-all-start.3 = ((f32[32,1,512]{2,1,0:T(1,128)}), f32[32,1,512]{2,1,0:T(1,128)S(1)}, u32[]{:S(2)}, u32[]{:S(2)}) async-start(f32[32,1,512]{2,1,0:T(1,128)} %broadcast_in_dim.61), calls=%async_computation.3 | async-start | bytes 131072 | tf_op jit(solution)/shard_map/all_to_all | solution.py:97
where the time goes:
time: 63.2 us; the launch traced here: 62.8 us
  waiting for transfers between devices  22.4 us (35%)
  starting transfers between devices  13.3 us (21%)
  blocking collectives  11.2 us (18%)
  other arithmetic  7.95 us (13%)
  local copies, waits for them, and re-layouts  6.78 us (11%)
  between operations  0.94 us (1%)
    all_to_all x1, blocking collectives, exchange(): got = lax.all_to_all(parcel, ('grid', 'mem'), 0, 0, tiled=True)  11.2 us
    all_to_all x1, waiting for transfers between devices, local_by_level(): got = lax.all_to_all(packed, 'grid', 1, 2, tiled=True)[:, 0]  10.4 us
    all_to_all x1, waiting for transfers between devices, exchange(): got = lax.all_to_all(parcel, ('grid', 'mem'), 0, 0, tiled=True)  7.41 us
    all_to_all x1, starting transfers between devices, local_by_level(): got = lax.all_to_all(packed, 'grid', 1, 2, tiled=True)[:, 0]  7.28 us
    all_to_all x1, waiting for transfers between devices, mem_total(): lax.all_to_all(jnp.broadcast_to(part, (mem_size,) + part.shape), 'mem', 0...  4.55 us
    all_to_all x1, starting transfers between devices, mem_total(): lax.all_to_all(jnp.broadcast_to(part, (mem_size,) + part.shape), 'mem', 0...  3.33 us
    all_to_all x1, starting transfers between devices, exchange(): got = lax.all_to_all(parcel, ('grid', 'mem'), 0, 0, tiled=True)  2.7 us
    unnamed x10, local copies, waits for them, and re-layouts  1.75 us
  transfers between devices with their start and end apart: 3, of which 3 were waited for; matrix products, arithmetic and copies ran while one was open for 1% of the time, Pallas kernels for 0%

commit v1 on v0

--- a/solution.py
+++ b/solution.py
@@ -6,6 +6,22 @@
 PASSES = 2
 ITERS = 2
 diffusion = 0.25
+
+
+def pairwise_exchange(shard, axis, split, join):
+    ways, here = (lax.axis_size(axis), lax.axis_index(axis))
+    width = shard.shape[split] // ways
+    lengths = list(shard.shape)
+    lengths[split] = width
+    height = lengths[join]
+    lengths[join] = height * ways
+    full = jnp.zeros(lengths, shard.dtype)
+    for mask in range(ways):
+        part = lax.dynamic_slice_in_dim(shard, (here ^ mask) * width, width, axis=split)
+        if mask:
+            part = lax.ppermute(part, axis, [(d, d ^ mask) for d in range(ways)])
+        full = lax.dynamic_update_slice_in_dim(full, part, (here ^ mask) * height, axis=join)
+    return full
 
 
 def padded(value, sides, width):
@@ -123,7 +139,7 @@
     low = rest - middle
     parts = jnp.stack([high, middle, low]).astype(jnp.bfloat16)
     packed = jnp.repeat(jnp.concatenate([members, counts, parts], axis=0), copies, axis=1)
-    got = lax.all_to_all(packed, "grid", 1, 2, tiled=True)[:, 0]
+    got = pairwise_exchange(packed, "grid", 1, 2)[:, 0]
     split = got[count + 1 :].astype(jnp.float32)
     innov = split[0] + split[1] + split[2]
     precision = lax.dynamic_index_in_dim(obs_precision, level, 0, keepdims=False)

time: 63.2 us -> 69.1 us (1.093)
  starting transfers between devices: 13.3 us -> 19.8 us
  waiting for transfers between devices: 22.4 us -> 19.3 us
  blocking collectives: 11.2 us -> 13.4 us
    ppermute x0 -> x7, starting transfers between devices: none -> 13.8 us  [pairwise_exchange(): part = lax.ppermute(part, axis, [(d, d ^ mask) for d in range(ways)])]
    all_to_all x1 -> x0, waiting for transfers between devices: 10.4 us -> none  [local_by_level(): got = lax.all_to_all(packed, 'grid', 1, 2, tiled=True)[:, 0]]
    ppermute x0 -> x7, waiting for transfers between devices: none -> 7.29 us  [pairwise_exchange(): part = lax.ppermute(part, axis, [(d, d ^ mask) for d in range(ways)])]
    all_to_all x1 -> x0, starting transfers between devices: 7.28 us -> none  [local_by_level(): got = lax.all_to_all(packed, 'grid', 1, 2, tiled=True)[:, 0]]
    all_to_all x1, blocking collectives: 11.2 us -> 13.4 us  [exchange(): got = lax.all_to_all(parcel, ('grid', 'mem'), 0, 0, tiled=True)]
    convert_element_type x1, other arithmetic: 0.77 us -> 0.01 us  [local_by_level(): observed_count.astype(jnp.bfloat16)]
    broadcast_in_dim x1, local copies, waits for them, and re-layouts: 0.94 us -> 0.21 us  [local_by_level(): jnp.repeat(jnp.concatenate([members, counts, parts], axis=0), copies, axi...]
    unnamed x10 -> x12, local copies, waits for them, and re-layouts: 1.75 us -> 2.42 us
  transfers between devices with their start and end apart: 3 -> 9, of which waited for: 3 -> 5; matrix products, arithmetic and copies ran while one was open for 1% -> 2% of each run, Pallas kernels for 0% -> 0%
where the time goes in v1:
time: 69.1 us; the launch traced here: 68.7 us
  starting transfers between devices  19.8 us (29%)
  waiting for transfers between devices  19.3 us (28%)
  blocking collectives  13.4 us (19%)
  other arithmetic  7.79 us (11%)
  local copies, waits for them, and re-layouts  6.89 us (10%)
  between operations  1.21 us (2%)
    ppermute x7, starting transfers between devices, pairwise_exchange(): part = lax.ppermute(part, axis, [(d, d ^ mask) for d in range(ways)])  13.8 us
    all_to_all x1, blocking collectives, exchange(): got = lax.all_to_all(parcel, ('grid', 'mem'), 0, 0, tiled=True)  13.4 us
    all_to_all x1, waiting for transfers between devices, exchange(): got = lax.all_to_all(parcel, ('grid', 'mem'), 0, 0, tiled=True)  7.41 us
    ppermute x7, waiting for transfers between devices, pairwise_exchange(): part = lax.ppermute(part, axis, [(d, d ^ mask) for d in range(ways)])  7.29 us
    all_to_all x1, waiting for transfers between devices, mem_total(): lax.all_to_all(jnp.broadcast_to(part, (mem_size,) + part.shape), 'mem', 0...  4.55 us
    all_to_all x1, starting transfers between devices, mem_total(): lax.all_to_all(jnp.broadcast_to(part, (mem_size,) + part.shape), 'mem', 0...  3.33 us
    all_to_all x1, starting transfers between devices, exchange(): got = lax.all_to_all(parcel, ('grid', 'mem'), 0, 0, tiled=True)  2.7 us
    unnamed x12, local copies, waits for them, and re-layouts  2.42 us
  transfers between devices with their start and end apart: 9, of which 5 were waited for; matrix products, arithmetic and copies ran while one was open for 2% of the time, Pallas kernels for 0%

profile of v1, /device:TPU:0, one launch (start us, length us, event | category | flops | bytes accessed | tf_op | source)
XLA Modules:
  0.0 68.7 jit_solution(4478329065446709864)
XLA Ops:
  0.7 0.7 copy-done.2
  1.4 1.0 %constant_dynamic-update-slice_fusion.4 = bf16[24,4,2,512]{3,2,1,0:T(2,128)(2,1)S(1)} fusion(bf16[20,4,2,512]{3,2,1,0:T(2,128)(2,1)} %param.4), kind=kLoop, calls=%fused_computation.151 | loop fusion | bytes 327680
  3.2 6.1 %collective-permute-start.6 = (bf16[24,1,2,512]{3,2,0,1:T(2,128)(2,1)S(1)}, bf16[24,1,2,512]{3,2,0,1:T(2,128)(2,1)S(1)}, u32[]{:S(2)}, u32[]{:S(2)}) collective-permute-start(bf16[24,1,2,512]{3,2,0,1:T(2,128)(2,1)S(1)} %get-tuple-element.17), channel_id=1, source_target_pairs={{0,28},{4,24},{8,20},{12,16},{16,12},{20,8},{24,4},{28,0},{1,29},{... | collective-permute-start | bytes 147464 | tf_op jit(solution)/shard_map/ppermute | solution.py:22
  9.4 0.8 %collective-permute-start.4 = (bf16[24,1,2,512]{3,2,0,1:T(2,128)(2,1)S(1)}, bf16[24,1,2,512]{3,2,0,1:T(2,128)(2,1)S(1)}, u32[]{:S(2)}, u32[]{:S(2)}) collective-permute-start(bf16[24,1,2,512]{3,2,0,1:T(2,128)(2,1)S(1)} %get-tuple-element.19), channel_id=1, source_target_pairs={{0,20},{4,16},{8,28},{12,24},{16,4},{20,0},{24,12},{28,8},{1,21},{... | collective-permute-start | bytes 147464 | tf_op jit(solution)/shard_map/ppermute | solution.py:22
  10.2 2.0 %collective-permute-start.3 = (bf16[24,1,2,512]{3,2,0,1:T(2,128)(2,1)S(1)}, bf16[24,1,2,512]{3,2,0,1:T(2,128)(2,1)S(1)}, u32[]{:S(2)}, u32[]{:S(2)}) collective-permute-start(bf16[24,1,2,512]{3,2,0,1:T(2,128)(2,1)S(1)} %get-tuple-element.20), channel_id=1, source_target_pairs={{0,16},{4,20},{8,24},{12,28},{16,0},{20,4},{24,8},{28,12},{1,17},{... | collective-permute-start | bytes 147464 | tf_op jit(solution)/shard_map/ppermute | solution.py:22
  12.2 1.6 %collective-permute-start = (bf16[24,1,2,512]{3,2,0,1:T(2,128)(2,1)S(1)}, bf16[24,1,2,512]{3,2,0,1:T(2,128)(2,1)S(1)}, u32[]{:S(2)}, u32[]{:S(2)}) collective-permute-start(bf16[24,1,2,512]{3,2,0,1:T(2,128)(2,1)S(1)} %get-tuple-element.23), channel_id=1, source_target_pairs={{0,4},{4,0},{8,12},{12,8},{16,20},{20,16},{24,28},{28,24},{1,5},{5... | collective-permute-start | bytes 147464 | tf_op jit(solution)/shard_map/ppermute | solution.py:22
  14.1 0.6 copy-done.3
  14.7 0.6 dynamic_slice.55
  15.3 1.5 %collective-permute-done = bf16[24,1,2,512]{3,2,0,1:T(2,128)(2,1)S(1)} collective-permute-done((bf16[24,1,2,512]{3,2,0,1:T(2,128)(2,1)S(1)}, bf16[24,1,2,512]{3,2,0,1:T(2,128)(2,1)S(1)}, u32[]{:S(2)}, u32[]{:S(2)}) %collective-permute-start) | collective-permute-done | bytes 49184 | tf_op jit(solution)/shard_map/ppermute | solution.py:22
  16.8 0.9 %collective-permute-start.1 = (bf16[24,1,2,512]{3,2,0,1:T(2,128)(2,1)S(1)}, bf16[24,1,2,512]{3,2,0,1:T(2,128)(2,1)S(1)}, u32[]{:S(2)}, u32[]{:S(2)}) collective-permute-start(bf16[24,1,2,512]{3,2,0,1:T(2,128)(2,1)S(1)} %get-tuple-element.22), channel_id=1, source_target_pairs={{0,8},{4,12},{8,0},{12,4},{16,24},{20,28},{24,16},{28,20},{1,9},{5... | collective-permute-start | bytes 147464 | tf_op jit(solution)/shard_map/ppermute | solution.py:22
  17.8 3.1 %collective-permute-done.1 = bf16[24,1,2,512]{3,2,0,1:T(2,128)(2,1)S(1)} collective-permute-done((bf16[24,1,2,512]{3,2,0,1:T(2,128)(2,1)S(1)}, bf16[24,1,2,512]{3,2,0,1:T(2,128)(2,1)S(1)}, u32[]{:S(2)}, u32[]{:S(2)}) %collective-permute-start.1) | collective-permute-done | bytes 49184 | tf_op jit(solution)/shard_map/ppermute | solution.py:22
  20.9 2.2 %collective-permute-start.2 = (bf16[24,1,2,512]{3,2,0,1:T(2,128)(2,1)S(1)}, bf16[24,1,2,512]{3,2,0,1:T(2,128)(2,1)S(1)}, u32[]{:S(2)}, u32[]{:S(2)}) collective-permute-start(bf16[24,1,2,512]{3,2,0,1:T(2,128)(2,1)S(1)} %get-tuple-element.21), channel_id=1, source_target_pairs={{0,12},{4,8},{8,4},{12,0},{16,28},{20,24},{24,20},{28,16},{1,13},{... | collective-permute-start | bytes 147464 | tf_op jit(solution)/shard_map/ppermute | solution.py:22
  23.2 2.7 %collective-permute-done.2 = bf16[24,1,2,512]{3,2,0,1:T(2,128)(2,1)S(1)} collective-permute-done((bf16[24,1,2,512]{3,2,0,1:T(2,128)(2,1)S(1)}, bf16[24,1,2,512]{3,2,0,1:T(2,128)(2,1)S(1)}, u32[]{:S(2)}, u32[]{:S(2)}) %collective-permute-start.2) | collective-permute-done | bytes 49184 | tf_op jit(solution)/shard_map/ppermute | solution.py:22
  26.4 0.7 convert_multiply_fusion.4
  27.1 0.3 fusion.28
  27.6 0.9 %fusion.23 = f32[20,16,512]{2,1,0:T(8,128)S(1)} fusion(f32[20,16,512]{2,1,0:T(8,128)S(1)} %fusion.28, f32[20,16,2]{2,1,0:T(8,128)S(1)} %get-tuple-element.14, f32[20,16,2]{2,1,0:T(8,128)S(1)} %get-tuple-element.13), kind=kLoop, calls=%fused_computation.59 | loop fusion | flops 1802240 | bytes 1315840 | tf_op jit(solution)/shard_map/add | solution.py:103
  28.5 0.3 fusion.34
  28.9 0.9 %fusion.57 = f32[16,512]{1,0:T(8,128)S(1)} fusion(f32[20,16,2]{2,1,0:T(8,128)S(1)} %get-tuple-element.12, f32[20,16,512]{2,1,0:T(8,128)S(1)} %fusion.34, f32[20,16,2]{2,1,0:T(8,128)S(1)} %get-tuple-element.11, bf16[20,16,512]{2,1,0:T(8,128)(2,1)S(1)} %slice.240), kind=kLoop, calls=%fused_computation.101 | loop fusion | flops 2285568 | bytes 1020928 | tf_op jit(solution)/shard_map/reduce_sum | solution.py:169
  29.8 0.7 broadcast_in_dim.58
  30.5 3.3 %all-to-all-start = ((f32[4,16,512]{2,1,0:T(8,128)}), f32[4,16,512]{2,1,0:T(8,128)S(1)}, u32[]{:S(2)}, u32[]{:S(2)}) async-start(f32[4,16,512]{2,1,0:T(8,128)} %broadcast_in_dim.58), calls=%async_computation | async-start | bytes 262144 | tf_op jit(solution)/shard_map/all_to_all | solution.py:122
  33.9 4.5 %all-to-all-done = f32[4,16,512]{2,1,0:T(8,128)S(1)} async-done(((f32[4,16,512]{2,1,0:T(8,128)}), f32[4,16,512]{2,1,0:T(8,128)S(1)}, u32[]{:S(2)}, u32[]{:S(2)}) %all-to-all-start) | async-done | bytes 131104 | tf_op jit(solution)/shard_map/all_to_all | solution.py:122
  38.4 0.7 fusion.62
  39.2 0.3 fusion.40
  39.6 0.9 %fusion.11 = f32[20,16,512]{2,1,0:T(8,128)S(1)} fusion(f32[20,16,512]{2,1,0:T(8,128)S(1)} %fusion.23, f32[20,16,512]{2,1,0:T(8,128)S(1)} %fusion.40, f32[20,16,2]{2,1,0:T(8,128)S(1)} %get-tuple-element.10, f32[20,16,2]{2,1,0:T(8,128)S(1)} %get-tuple-element.9), kind=kLoop, calls=%fused_computation.47 | loop fusion | flops 1966080 | bytes 1971200 | tf_op jit(solution)/shard_map/add | solution.py:170
  40.5 0.3 fusion.46
  41.0 0.9 %fusion.58 = f32[16,512]{1,0:T(8,128)S(1)} fusion(f32[20,16,2]{2,1,0:T(8,128)S(1)} %get-tuple-element.8, f32[20,16,512]{2,1,0:T(8,128)S(1)} %fusion.46, f32[20,16,2]{2,1,0:T(8,128)S(1)} %get-tuple-element.7, bf16[20,16,512]{2,1,0:T(8,128)(2,1)S(1)} %slice.240), kind=kLoop, calls=%fused_computation.102 | loop fusion | flops 2285568 | bytes 1020928 | tf_op jit(solution)/shard_map/reduce_sum | solution.py:171
  42.2 13.4 %all_to_all.23 = f32[32,1,1280]{2,1,0:T(1,128)S(1)} all-to-all(f32[32,1,1280]{2,1,0:T(1,128)S(1)} %all_to_all.16), channel_id=1, replica_groups=mesh['grid'=8,'mem'=4] {'grid','mem'}, dimensions={0} | all-to-all | bytes 327680 | tf_op jit(solution)/shard_map/all_to_all | solution.py:113
  56.2 0.7 broadcast_in_dim.62
  56.9 2.7 %all-to-all-start.2 = ((f32[32,1,512]{2,1,0:T(1,128)}), f32[32,1,512]{2,1,0:T(1,128)S(1)}, u32[]{:S(2)}, u32[]{:S(2)}) async-start(f32[32,1,512]{2,1,0:T(1,128)} %broadcast_in_dim.62), calls=%async_computation.2 | async-start | bytes 131072 | tf_op jit(solution)/shard_map/all_to_all | solution.py:113
  59.6 7.4 %all-to-all-done.2 = f32[32,1,512]{2,1,0:T(1,128)S(1)} async-done(((f32[32,1,512]{2,1,0:T(1,128)}), f32[32,1,512]{2,1,0:T(1,128)S(1)}, u32[]{:S(2)}, u32[]{:S(2)}) %all-to-all-start.2) | async-done | bytes 65568 | tf_op jit(solution)/shard_map/all_to_all | solution.py:113
  67.3 0.8 %add_convert_fusion = bf16[20,4,2,512]{3,2,1,0:T(2,128)(2,1)} fusion(bf16[20,4,2,512]{3,2,1,0:T(2,128)(2,1)S(1)} %copy-done, f32[4,2,512]{2,1,0:T(2,128)S(1)} %multiply_add_fusion), kind=kLoop, calls=%fused_computation.105 | loop fusion | flops 245760 | bytes 344064 | tf_op jit(solution)/shard_map/convert_element_type | solution.py:210
  68.1 0.6 constant_dynamic-slice_fusion
  (67 shorter events, 3.3 us)
Async XLA Ops:
  0.7 0.7 %copy-start.2 = (s32[2,512]{1,0:T(2,128)S(1)}, s32[2,512]{1,0:T(2,128)}, u32[]{:S(2)}) copy-start(s32[2,512]{1,0:T(2,128)} %param.6) | copy-start | bytes 12292
  1.4 1.1 %copy-start.1 = (f32[4,2,512]{2,1,0:T(2,128)S(1)}, f32[4,2,512]{2,1,0:T(2,128)}, u32[]{:S(2)}) copy-start(f32[4,2,512]{2,1,0:T(2,128)} %param.5) | copy-start | bytes 49156
  3.2 23.1 %collective-permute-start.6 = (bf16[24,1,2,512]{3,2,0,1:T(2,128)(2,1)S(1)}, bf16[24,1,2,512]{3,2,0,1:T(2,128)(2,1)S(1)}, u32[]{:S(2)}, u32[]{:S(2)}) collective-permute-start(bf16[24,1,2,512]{3,2,0,1:T(2,128)(2,1)S(1)} %get-tuple-element.17), channel_id=1, source_target_pairs={{0,28},{4,24},{8,20},{12,16},{16,12},{20,8},{24,4},{28,0},{1,29},{... | collective-permute-start | bytes 147464 | tf_op jit(solution)/shard_map/ppermute | solution.py:22
  9.2 16.9 %collective-permute-start.5 = (bf16[24,1,2,512]{3,2,0,1:T(2,128)(2,1)S(1)}, bf16[24,1,2,512]{3,2,0,1:T(2,128)(2,1)S(1)}, u32[]{:S(2)}, u32[]{:S(2)}) collective-permute-start(bf16[24,1,2,512]{3,2,0,1:T(2,128)(2,1)S(1)} %get-tuple-element.18), channel_id=1, source_target_pairs={{0,24},{4,28},{8,16},{12,20},{16,8},{20,12},{24,0},{28,4},{1,25},{... | collective-permute-start | bytes 147464 | tf_op jit(solution)/shard_map/ppermute | solution.py:22
  9.4 16.6 %collective-permute-start.4 = (bf16[24,1,2,512]{3,2,0,1:T(2,128)(2,1)S(1)}, bf16[24,1,2,512]{3,2,0,1:T(2,128)(2,1)S(1)}, u32[]{:S(2)}, u32[]{:S(2)}) collective-permute-start(bf16[24,1,2,512]{3,2,0,1:T(2,128)(2,1)S(1)} %get-tuple-element.19), channel_id=1, source_target_pairs={{0,20},{4,16},{8,28},{12,24},{16,4},{20,0},{24,12},{28,8},{1,21},{... | collective-permute-start | bytes 147464 | tf_op jit(solution)/shard_map/ppermute | solution.py:22
  10.2 15.7 %collective-permute-start.3 = (bf16[24,1,2,512]{3,2,0,1:T(2,128)(2,1)S(1)}, bf16[24,1,2,512]{3,2,0,1:T(2,128)(2,1)S(1)}, u32[]{:S(2)}, u32[]{:S(2)}) collective-permute-start(bf16[24,1,2,512]{3,2,0,1:T(2,128)(2,1)S(1)} %get-tuple-element.20), channel_id=1, source_target_pairs={{0,16},{4,20},{8,24},{12,28},{16,0},{20,4},{24,8},{28,12},{1,17},{... | collective-permute-start | bytes 147464 | tf_op jit(solution)/shard_map/ppermute | solution.py:22
  12.2 4.5 %collective-permute-start = (bf16[24,1,2,512]{3,2,0,1:T(2,128)(2,1)S(1)}, bf16[24,1,2,512]{3,2,0,1:T(2,128)(2,1)S(1)}, u32[]{:S(2)}, u32[]{:S(2)}) collective-permute-start(bf16[24,1,2,512]{3,2,0,1:T(2,128)(2,1)S(1)} %get-tuple-element.23), channel_id=1, source_target_pairs={{0,4},{4,0},{8,12},{12,8},{16,20},{20,16},{24,28},{28,24},{1,5},{5... | collective-permute-start | bytes 147464 | tf_op jit(solution)/shard_map/ppermute | solution.py:22
  14.1 0.7 copy-start.3
  16.8 4.1 %collective-permute-start.1 = (bf16[24,1,2,512]{3,2,0,1:T(2,128)(2,1)S(1)}, bf16[24,1,2,512]{3,2,0,1:T(2,128)(2,1)S(1)}, u32[]{:S(2)}, u32[]{:S(2)}) collective-permute-start(bf16[24,1,2,512]{3,2,0,1:T(2,128)(2,1)S(1)} %get-tuple-element.22), channel_id=1, source_target_pairs={{0,8},{4,12},{8,0},{12,4},{16,24},{20,28},{24,16},{28,20},{1,9},{5... | collective-permute-start | bytes 147464 | tf_op jit(solution)/shard_map/ppermute | solution.py:22
  20.9 5.0 %collective-permute-start.2 = (bf16[24,1,2,512]{3,2,0,1:T(2,128)(2,1)S(1)}, bf16[24,1,2,512]{3,2,0,1:T(2,128)(2,1)S(1)}, u32[]{:S(2)}, u32[]{:S(2)}) collective-permute-start(bf16[24,1,2,512]{3,2,0,1:T(2,128)(2,1)S(1)} %get-tuple-element.21), channel_id=1, source_target_pairs={{0,12},{4,8},{8,4},{12,0},{16,28},{20,24},{24,20},{28,16},{1,13},{... | collective-permute-start | bytes 147464 | tf_op jit(solution)/shard_map/ppermute | solution.py:22
  30.5 7.9 %all-to-all-start = ((f32[4,16,512]{2,1,0:T(8,128)}), f32[4,16,512]{2,1,0:T(8,128)S(1)}, u32[]{:S(2)}, u32[]{:S(2)}) async-start(f32[4,16,512]{2,1,0:T(8,128)} %broadcast_in_dim.58), calls=%async_computation | async-start | bytes 262144 | tf_op jit(solution)/shard_map/all_to_all | solution.py:122
  56.9 10.4 %copy-start = (bf16[20,4,2,512]{3,2,1,0:T(2,128)(2,1)S(1)}, bf16[20,4,2,512]{3,2,1,0:T(2,128)(2,1)}, u32[]{:S(2)}) copy-start(bf16[20,4,2,512]{3,2,1,0:T(2,128)(2,1)} %param.4) | copy-start | bytes 491524
  56.9 10.1 %all-to-all-start.2 = ((f32[32,1,512]{2,1,0:T(1,128)}), f32[32,1,512]{2,1,0:T(1,128)S(1)}, u32[]{:S(2)}, u32[]{:S(2)}) async-start(f32[32,1,512]{2,1,0:T(1,128)} %broadcast_in_dim.62), calls=%async_computation.2 | async-start | bytes 131072 | tf_op jit(solution)/shard_map/all_to_all | solution.py:113
